TPU v7x, 256 devices: a whole 4x4x8 slice. The times are simulated.
256 devices in a mesh: row: 8 (over z), col: 32 (over y, x, core).
Axes of the slice: x: 4, y: 4, z: 8, core: 2. Of those that a mesh axis runs over, the one named last changes fastest.
Arguments:
- hidden_in: bfloat16 [1024, 2304], P('row', 'col'), may hold values from -40 to 40
- attn_gain: float32 [2304], P('col'), may hold values from 0.1 to 1.9
- qkv_weight: bfloat16 [2304, 6912], P('col'), may hold values from -0.125 to 0.125
- out_weight: bfloat16 [2304, 2304], P(None, 'col'), may hold values from -0.125 to 0.125
- moe_gain: float32 [2304], P('col'), may hold values from 0.1 to 1.9
- router_weight: float32 [2304, 8], P('col'), may hold values from -0.125 to 0.125
- expert_gate: bfloat16 [8, 2304, 5760], P('row', None, 'col'), may hold values from -0.125 to 0.125
- expert_up: bfloat16 [8, 2304, 5760], P('row', None, 'col'), may hold values from -0.125 to 0.125
- expert_down: bfloat16 [8, 5760, 2304], P('row', 'col'), may hold values from -0.078125 to 0.078125
- cache_keys: bfloat16 [2048, 64, 2304], P(('row', 'col')), may hold values from -400 to 400
- cache_values: bfloat16 [2048, 64, 2304], P(('row', 'col')), may hold values from -12 to 12
- block_table: int32 [8, 4, 64], P('row'), may hold values from 0 to 2047, as said below
- prefix_lengths: int32 [8, 4], P('row'), may hold values from 1024 to 4096, as said below
- prompt_lengths: int32 [8, 4], P('row'), may hold values from 1 to 64, 128 in all within a row
- routed_experts: int32 [1024, 2], P('row'), may hold values from 0 to 7, all different within a row; in each aligned block of 128 rows (0 to 127, 128 to 255, ...) at most 64 rows name the same one
Outputs:
- attn_out: bfloat16 [1024, 2304], P('row', 'col')
- moe_out: bfloat16 [1024, 2304], P('row', 'col')
- layer_out: bfloat16 [1024, 2304], P('row', 'col')
Inputs may be any that keep to these rules, and one draw needn't show every extreme that they name: `block_table`: entry [g, q, j] lies among the 8 pages that begin at (g * 32 + j % 32) * 8; the entries that fall among the same 8 pages are distinct. `prefix_lengths`: some request has exactly 4096 cached tokens. `prompt_lengths`: the 4 lengths of a group sum to 128; the longest of each group is exactly 64. `routed_experts`: the 2 experts of a token differ; among the tokens of one group no expert is named more than 64 times, and in some group an expert reaches 64; every expert is named by some token.
All inputs are finite; a program needn't handle non-finite values.
Results may differ from a plain program's by a relative error of at most 0.02.
The roundings to bfloat16 on the way count: a program that leaves them out, or rounds other values in their place, can miss the bound.
Values may be sent and summed in bfloat16 or wider, within the bound.
No kernel may reach another device: no remote copies, remote signals or barrier semaphores. Data moves between devices by JAX's collectives and lax.ppermute only.
A program may use at most 192 MiB of HBM per device.

v0:
```python
import math
import jax
import jax.numpy as jnp
from jax import lax
from jax.sharding import PartitionSpec as P

D = 2304
HEAD_DIM = 64
TOP = 2
norm_epsilon = 1e-05
residual_scale = 1.4 / math.sqrt(40.0)
rotary_base = 10000.0
masked_score = -1e30


def merged(value, axis, join):
    pieces = jax.tree.map(lambda part: lax.all_gather(part, axis), value)
    head = jax.tree.map(lambda part: part[0], pieces)
    tail = jax.tree.map(lambda part: part[1:], pieces)
    running, _ = lax.scan(lambda running, slab: (join(running, slab), None), head, tail)
    return running


def rotate(values, positions, head_dim):
    row_count = values.shape[0]
    head_count = values.shape[1] // head_dim
    half_dim = head_dim // 2
    frequency = rotary_base ** (-2.0 * jnp.arange(half_dim, dtype=jnp.float32) / head_dim)
    angles = positions.astype(jnp.float32)[:, None] * frequency[None, :]
    cosine = jnp.cos(angles)[:, None, :]
    sine_part = jnp.sin(angles)[:, None, :]
    shaped = values.reshape(row_count, head_count, head_dim)
    first_half = shaped[:, :, :half_dim]
    second_half = shaped[:, :, half_dim:]
    turned = jnp.concatenate(
        [
            first_half * cosine - second_half * sine_part,
            second_half * cosine + first_half * sine_part,
        ],
        axis=2,
    )
    return turned.reshape(row_count, head_count * head_dim)


def token_layout(prompt_row, prefix_row, row_count):
    run_ends = jnp.cumsum(prompt_row, dtype=jnp.int32)
    starts = run_ends - prompt_row
    offsets = jnp.arange(row_count, dtype=jnp.int32)
    request = jnp.sum(
        (offsets[:, None] >= run_ends[None, :]).astype(jnp.int32), axis=1, dtype=jnp.int32
    )
    member = request[:, None] == jnp.arange(prompt_row.shape[0], dtype=jnp.int32)[None, :]
    start_of = jnp.sum(jnp.where(member, starts[None, :], 0), axis=1, dtype=jnp.int32)
    prefix_of = jnp.sum(jnp.where(member, prefix_row[None, :], 0), axis=1, dtype=jnp.int32)
    return (request, prefix_of + offsets - start_of)


def rescale(summed, factor):
    group_count, row_count, feature_width = summed.shape
    group_size = factor.shape[1]
    shaped = summed.reshape(group_count, row_count, group_size, feature_width // group_size)
    shaped = shaped * jnp.transpose(factor, (0, 2, 1))[:, :, :, None]
    return shaped.reshape(group_count, row_count, feature_width)


def divide_rows(summed, total_weight):
    group_count, row_count, feature_width = summed.shape
    group_size = total_weight.shape[1]
    shaped = summed.reshape(group_count, row_count, group_size, feature_width // group_size)
    shaped = shaped / jnp.transpose(total_weight, (0, 2, 1))[:, :, :, None]
    return shaped.reshape(group_count, row_count, feature_width)


def combine_parts(earlier_part, later_part):
    largest = jnp.maximum(earlier_part[0], later_part[0])
    factor_one = jnp.exp(earlier_part[0] - largest)
    factor_two = jnp.exp(later_part[0] - largest)
    total_weight = earlier_part[1] * factor_one + later_part[1] * factor_two
    summed = rescale(earlier_part[2], factor_one) + rescale(later_part[2], factor_two)
    return (largest, total_weight, summed)


def on_device(
    hidden_in,
    attn_gain,
    qkv_weight,
    out_weight,
    moe_gain,
    router_weight,
    expert_gate,
    expert_up,
    expert_down,
    cache_keys,
    cache_values,
    block_table,
    prefix_lengths,
    prompt_lengths,
    routed_experts,
):
    col_count = lax.axis_size("col")
    row_devices = lax.axis_size("row")
    col_index = lax.axis_index("col")
    row_index = lax.axis_index("row")
    tok_rows = hidden_in.shape[0]
    feature_width = hidden_in.shape[1]
    head_total = out_weight.shape[0]
    head_count = head_total // HEAD_DIM
    key_share = tok_rows // col_count
    request, position = token_layout(prompt_lengths[0], prefix_lengths[0], tok_rows)
    own_start = col_index * key_share
    key_position = lax.dynamic_slice_in_dim(position, own_start, key_share)
    key_request = lax.dynamic_slice_in_dim(request, own_start, key_share)
    residual = hidden_in.astype(jnp.float32)
    squares = lax.psum(jnp.sum(residual * residual, axis=1), "col")
    scale_one = lax.rsqrt(squares / D + norm_epsilon)
    normed = (residual * scale_one[:, None] * attn_gain[None, :]).astype(jnp.bfloat16)
    query_part = jnp.dot(normed, qkv_weight[:, :head_total], preferred_element_type=jnp.float32)
    query_sum = lax.psum(query_part, "col")
    queries = (rotate(query_sum, position, HEAD_DIM) * HEAD_DIM ** (-0.5)).astype(jnp.bfloat16)
    key_value = lax.psum_scatter(
        jnp.dot(normed, qkv_weight[:, head_total:], preferred_element_type=jnp.float32).astype(
            jnp.bfloat16
        ),
        "col",
        scatter_dimension=0,
        tiled=True,
    ).astype(jnp.float32)
    new_keys = rotate(key_value[:, :head_total], key_position, HEAD_DIM).astype(jnp.bfloat16)
    new_values = key_value[:, head_total:].astype(jnp.bfloat16)
    pool_size = cache_keys.shape[0]
    page_size = cache_keys.shape[1]
    req_count = block_table.shape[1]
    pages_each = block_table.shape[2] // col_count
    page_table = block_table[0].reshape(req_count, pages_each, col_count)
    own_pages = lax.dynamic_slice_in_dim(page_table, col_index, 1, 2).reshape(
        req_count * pages_each
    )
    pool_offset_begin = (row_index * col_count + col_index) * pool_size
    slot_ids = jnp.arange(pool_size, dtype=jnp.int32)
    entry_ids = jnp.arange(req_count * pages_each, dtype=jnp.int32)
    slot_match = (own_pages - pool_offset_begin)[None, :] == slot_ids[:, None]
    entry_request = entry_ids // pages_each
    entry_page = entry_ids % pages_each * col_count + col_index
    slot_request = jnp.sum(
        jnp.where(slot_match, entry_request[None, :], 0), axis=1, dtype=jnp.int32
    )
    slot_page = jnp.sum(jnp.where(slot_match, entry_page[None, :], 0), axis=1, dtype=jnp.int32)
    prefix_row = prefix_lengths[0]
    slot_prefix = jnp.sum(
        jnp.where(
            slot_request[:, None] == jnp.arange(req_count, dtype=jnp.int32)[None, :],
            prefix_row[None, :],
            0,
        ),
        axis=1,
        dtype=jnp.int32,
    )
    cache_position = (
        slot_page[:, None] * page_size + jnp.arange(page_size, dtype=jnp.int32)[None, :]
    )
    cache_live = (
        (cache_position < slot_prefix[:, None]).astype(jnp.int32).reshape(pool_size * page_size)
    )
    cache_request = jnp.broadcast_to(slot_request[:, None], (pool_size, page_size)).reshape(
        pool_size * page_size
    )
    cache_mask = (request[:, None] == cache_request[None, :]) & (cache_live[None, :] > 0)
    fresh_mask = (request[:, None] == key_request[None, :]) & (
        key_position[None, :] <= position[:, None]
    )
    group_size = math.gcd(head_count, 4)
    group_count = head_count // group_size
    query_heads = queries.reshape(tok_rows, head_count, HEAD_DIM)
    cached_key_heads = cache_keys.reshape(pool_size * page_size, head_count, HEAD_DIM)
    cached_value_heads = cache_values.reshape(pool_size * page_size, head_count, HEAD_DIM)
    fresh_key_heads = new_keys.reshape(key_share, head_count, HEAD_DIM)
    fresh_value_heads = new_values.reshape(key_share, head_count, HEAD_DIM)

    def head_group(group_index):
        first_head = group_index * group_size
        query_piece = lax.dynamic_slice_in_dim(query_heads, first_head, group_size, 1)
        key_piece = lax.dynamic_slice_in_dim(cached_key_heads, first_head, group_size, 1)
        value_piece = lax.dynamic_slice_in_dim(cached_value_heads, first_head, group_size, 1)
        fresh_key_piece = lax.dynamic_slice_in_dim(fresh_key_heads, first_head, group_size, 1)
        fresh_value_piece = lax.dynamic_slice_in_dim(fresh_value_heads, first_head, group_size, 1)
        score_matrix = jnp.einsum(
            "thd,khd->htk", query_piece, key_piece, preferred_element_type=jnp.float32
        )
        score_matrix = jnp.where(cache_mask[None], score_matrix, masked_score)
        fresh_scores = jnp.einsum(
            "thd,khd->htk", query_piece, fresh_key_piece, preferred_element_type=jnp.float32
        )
        fresh_scores = jnp.where(fresh_mask[None], fresh_scores, masked_score)
        largest = jnp.maximum(jnp.max(score_matrix, axis=2), jnp.max(fresh_scores, axis=2))
        cached_exp = jnp.where(cache_mask[None], jnp.exp(score_matrix - largest[:, :, None]), 0.0)
        fresh_exp = jnp.where(fresh_mask[None], jnp.exp(fresh_scores - largest[:, :, None]), 0.0)
        total_weight = jnp.sum(cached_exp, axis=2) + jnp.sum(fresh_exp, axis=2)
        summed = jnp.einsum(
            "htk,khd->thd",
            cached_exp.astype(jnp.bfloat16),
            value_piece,
            preferred_element_type=jnp.float32,
        )
        summed = summed + jnp.einsum(
            "htk,khd->thd",
            fresh_exp.astype(jnp.bfloat16),
            fresh_value_piece,
            preferred_element_type=jnp.float32,
        )
        return (largest, total_weight, summed.reshape(tok_rows, group_size * HEAD_DIM))

    largest, total_weight, summed = lax.map(head_group, jnp.arange(group_count, dtype=jnp.int32))
    largest, total_weight, summed = merged((largest, total_weight, summed), "col", combine_parts)
    attended = divide_rows(summed, total_weight).astype(jnp.bfloat16)
    projected = jnp.einsum(
        "gtx,gxo->to",
        attended,
        out_weight.reshape(group_count, group_size * HEAD_DIM, feature_width),
        preferred_element_type=jnp.float32,
    )
    attn_out = projected.astype(jnp.bfloat16)
    middle = (residual + residual_scale * attn_out.astype(jnp.float32)).astype(jnp.bfloat16)
    middle_wide = middle.astype(jnp.float32)
    squares_two = lax.psum(jnp.sum(middle_wide * middle_wide, axis=1), "col")
    scale_two = lax.rsqrt(squares_two / D + norm_epsilon)
    moe_normed_f = middle_wide * scale_two[:, None] * moe_gain[None, :]
    logits = lax.psum(jnp.dot(moe_normed_f, router_weight, precision=lax.Precision.HIGHEST), "col")
    moe_normed = moe_normed_f.astype(jnp.bfloat16)
    expert_local = expert_gate.shape[0]
    expert_total = expert_local * row_devices
    capacity = 2 * TOP * tok_rows // expert_total
    onehot_three = (
        routed_experts[:, :, None] == jnp.arange(expert_total, dtype=jnp.int32)[None, None, :]
    )
    selected_logits = jnp.sum(jnp.where(onehot_three, logits[:, None, :], 0.0), axis=2)
    first_gate = jax.nn.sigmoid(selected_logits[:, 0] - selected_logits[:, 1])
    gate_pair = jnp.stack([first_gate, 1.0 - first_gate], axis=1)
    onehot = onehot_three.astype(jnp.int32).reshape(tok_rows * TOP, expert_total)
    earlier = jnp.cumsum(onehot, axis=0, dtype=jnp.int32) - onehot
    slot_index = jnp.sum(earlier * onehot, axis=1, dtype=jnp.int32)
    target = routed_experts.reshape(tok_rows * TOP) * capacity + slot_index
    token_local = jnp.arange(tok_rows * TOP, dtype=jnp.int32) // TOP
    source = jnp.zeros((expert_total * capacity,), jnp.int32).at[target].set(token_local)
    filled = jnp.zeros((expert_total * capacity,), jnp.int32).at[target].set(1)
    outgoing = jnp.where(
        filled[:, None] > 0, moe_normed[source], jnp.zeros((), jnp.bfloat16)
    ).reshape(expert_total, capacity, feature_width)
    arrived = lax.all_to_all(outgoing, "row", split_axis=0, concat_axis=0, tiled=True)
    expert_rows = (
        arrived.reshape(row_devices, expert_local, capacity, feature_width)
        .transpose(1, 0, 2, 3)
        .reshape(expert_local, row_devices * capacity, feature_width)
    )
    feature_piece = lax.all_gather(expert_rows, "col", axis=2, tiled=True)
    gate_next = jnp.einsum(
        "erd,edf->erf", feature_piece, expert_gate, preferred_element_type=jnp.float32
    )
    up_next = jnp.einsum(
        "erd,edf->erf", feature_piece, expert_up, preferred_element_type=jnp.float32
    )
    hidden = (jax.nn.silu(gate_next) * up_next).astype(jnp.bfloat16)
    received_rows = hidden.shape[1]
    value_partial_sum = jnp.einsum(
        "efo,erf->oer", expert_down, hidden, preferred_element_type=jnp.float32
    )
    expert_out = lax.psum_scatter(
        value_partial_sum.reshape(
            lax.axis_size("col") * feature_width, expert_local * received_rows
        ).astype(jnp.bfloat16),
        "col",
        scatter_dimension=0,
        tiled=True,
    )
    returned = lax.all_to_all(
        expert_out.reshape(feature_width, expert_local, received_rows),
        "row",
        split_axis=2,
        concat_axis=1,
        tiled=True,
    )
    flat_back = returned.reshape(feature_width, expert_total * capacity)
    picked = (
        jnp.take(flat_back, target, axis=1)
        .astype(jnp.float32)
        .reshape(feature_width, tok_rows, TOP)
    )
    moe_columns = jnp.sum(picked * gate_pair[None, :, :], axis=2).astype(jnp.bfloat16)
    moe_out = moe_columns.T
    layer_out = (middle_wide + residual_scale * moe_out.astype(jnp.float32)).astype(jnp.bfloat16)
    return (attn_out, moe_out, layer_out)


def solution(mesh):
    in_specs = (
        P("row", "col"),
        P("col"),
        P("col", None),
        P(None, "col"),
        P("col"),
        P("col", None),
        P("row", None, "col"),
        P("row", None, "col"),
        P("row", "col", None),
        P(("row", "col"), None, None),
        P(("row", "col"), None, None),
        P("row", None, None),
        P("row", None),
        P("row", None),
        P("row", None),
    )
    out_specs = (P("row", "col"), P("row", "col"), P("row", "col"))
    return jax.shard_map(
        on_device, mesh=mesh, in_specs=in_specs, out_specs=out_specs, check_vma=False
    )
```

profile of v0, /device:TPU:2, one launch (start us, length us, event | category | flops | bytes accessed | tf_op | source)
XLA Modules:
  0.0 942.3 jit_solution(6926186442801343392)
XLA Ops:
  8.0 62.3 %psum.28 = f32[128]{0:T(128)S(1)} all-reduce(f32[128]{0:T(128)S(1)} %fusion.64), channel_id=1, replica_groups=mesh['row'=8,'col'=32] {'col'}, use_global_device_ids=true, to_apply=%region_1.2 | all-reduce | flops 128 | bytes 1024 | tf_op jit(solution)/shard_map/psum | solution.py:114
  70.3 2.7 convolution_convert_fusion
  77.7 5.0 reshape.454
  82.7 6.9 copy.162
  89.5 5.0 reshape.455
  94.5 6.7 copy.163
  102.5 88.4 %all-reduce.6.cloned.1.call-done = bf16[128,4608]{1,0:T(8,128)(2,1)} async-done(((bf16[128,4608]{1,0:T(8,128)(2,1)}), bf16[128,4608]{1,0:T(8,128)(2,1)}) %all-reduce.6.cloned.1.call-update) | async-done | bytes 1179664
  192.2 117.1 %all-reduce.4.cloned.1.call-done = f32[128,36,64]{0,2,1:T(8,128)} async-done(((f32[128,36,64]{0,2,1:T(8,128)}), f32[128,36,64]{0,2,1:T(8,128)}) %all-reduce.4.cloned.1.call-update) | async-done | bytes 1179664 | tf_op jit(solution)/shard_map/psum | solution.py:118
  310.9 51.9 %while.31 = (s32[]{:T(128)}, f32[9,4,128]{2,1,0:T(4,128)S(1)}, f32[9,4,128]{2,1,0:T(4,128)S(1)}, f32[9,128,256]{2,1,0:T(8,128)}, s32[9]{0:T(128)S(1)}, /*index=5...) while((s32[]{:T(128)}, f32[9,4,128]{2,1,0:T(4,128)S(1)}, ...), condition=%wide.region_16.17_spmd.clone.clone, body=%wide.region_11.16_spmd.clone.clone.sunk | while | flops 69911040 | bytes 5058339 | solution.py:212
  368.0 24.4 %all-gather = f32[288,4,128]{2,1,0:T(4,128)S(1)} all-gather(f32[9,4,128]{2,1,0:T(4,128)S(1)} %get-tuple-element.105), channel_id=2, replica_groups=mesh['row'=8,'col'=32] {'col'}, dimensions={0}, use_global_device_ids=true | all-gather | bytes 608256 | tf_op jit(solution)/shard_map/all_gather | solution.py:17
  392.5 25.6 %all-gather.1 = f32[288,4,128]{2,1,0:T(4,128)S(1)} all-gather(f32[9,4,128]{2,1,0:T(4,128)S(1)} %get-tuple-element.106), channel_id=3, replica_groups=mesh['row'=8,'col'=32] {'col'}, dimensions={0}, use_global_device_ids=true | all-gather | bytes 608256 | tf_op jit(solution)/shard_map/all_gather | solution.py:17
  418.2 76.0 %all-gather.8.cloned.1.call-done = f32[288,128,256]{2,1,0:T(8,128)} async-done(((f32[9,128,256]{2,1,0:T(8,128)}), f32[288,128,256]{2,1,0:T(8,128)}) %all-gather.8.cloned.1.call-update) | async-done | bytes 37748752 | tf_op jit(solution)/shard_map/all_gather | solution.py:17
  496.8 26.9 %slice.93 = f32[279,128,256]{2,1,0:T(8,128)} slice(f32[288,128,256]{2,1,0:T(8,128)} %all-gather.8.cloned.1.call-done), slice={[9:288], [0:128], [0:256]} | slice | bytes 73138176 | tf_op jit(solution)/shard_map/slice | solution.py:19
  523.7 168.2 %while.30 = (s32[]{:T(128)}, f32[9,4,128]{2,1,0:T(4,128)S(1)}, f32[9,4,128]{2,1,0:T(4,128)S(1)}, f32[9,128,256]{1,2,0:T(8,128)}, f32[31,9,4,128]{3,2,1,0:T(4,128...) while((s32[]{:T(128)}, f32[9,4,128]{2,1,0:T(4,128)S(1)}, ...), condition=%wide.region_18.19_spmd, body=%wide.region_17.18_spmd.sunk | while | flops 916994 | bytes 17676496 | solution.py:20
  531.9 2.6 fusion.111
  542.8 2.6 fusion.111
  548.2 2.6 fusion.111
  553.6 2.6 fusion.111
  559.1 2.6 fusion.111
  569.9 2.6 fusion.111
  580.8 2.6 fusion.111
  591.6 2.6 fusion.111
  602.5 2.6 fusion.111
  694.2 60.6 %psum.30 = f32[128]{0:T(128)S(1)} all-reduce(f32[128]{0:T(128)S(1)} %get-tuple-element.401), channel_id=1, replica_groups=mesh['row'=8,'col'=32] {'col'}, use_global_device_ids=true, to_apply=%region_24.25 | all-reduce | flops 128 | bytes 1024 | tf_op jit(solution)/shard_map/psum | solution.py:224
  756.5 15.9 %all_to_all.14 = bf16[8,64,72]{2,1,0:T(8,128)(2,1)S(1)} all-to-all(bf16[8,64,72]{2,1,0:T(8,128)(2,1)S(1)} %broadcast_select_fusion), channel_id=1, replica_groups=mesh['row'=8,'col'=32] {'row'}, dimensions={0} | all-to-all | bytes 147456 | tf_op jit(solution)/shard_map/all_to_all | solution.py:248
  773.2 44.9 %all-gather.6.cloned.1.call-done = bf16[1,512,2304]{1,2,0:T(8,128)(2,1)} async-done(((bf16[1,512,72]{1,2,0:T(8,128)(2,1)}), bf16[1,512,2304]{1,2,0:T(8,128)(2,1)}) %all-gather.6.cloned.1.call-update) | async-done | bytes 2359312 | tf_op jit(solution)/shard_map/all_gather | solution.py:254
  818.1 3.0 fusion.36
  821.2 3.4 fusion.33
  827.9 60.4 %psum.31 = f32[128,8]{0,1:T(8,128)S(1)} all-reduce(f32[128,8]{0,1:T(8,128)S(1)} %fusion.70), channel_id=1, replica_groups=mesh['row'=8,'col'=32] {'col'}, use_global_device_ids=true, to_apply=%region_27.28 | all-reduce | flops 1024 | bytes 8192 | tf_op jit(solution)/shard_map/psum | solution.py:227
  888.4 25.3 %reduce-scatter.4.cloned.1.call-done = bf16[72,512]{1,0:T(8,128)(2,1)} async-done(((bf16[2304,512]{1,0:T(8,128)(2,1)}), bf16[72,512]{1,0:T(8,128)(2,1)}) %reduce-scatter.4.cloned.1.call-update) | async-done | bytes 73744
  917.8 7.0 all-to-all-start.1
  925.0 8.3 all-to-all-done.1
  (687 shorter events, 219.2 us)
Async XLA Ops:
  7.2 814.0 %copy-start = (bf16[1,180,2304]{2,1,0:T(8,128)(2,1)S(1)}, bf16[1,180,2304]{2,1,0:T(8,128)(2,1)}, u32[]{:S(2)}) copy-start(bf16[1,180,2304]{2,1,0:T(8,128)(2,1)} %param.27) | copy-start | bytes 2488324
  7.2 183.7 %all-reduce.6.cloned.1.call-start = ((), (), s32[]{:S(2)}) async-start(), calls=%async_computation.7 | async-start | bytes 2359296
  70.3 2.9 copy-start.8
  70.3 2.9 copy-start.12
  73.1 2.9 copy-start.17
  73.1 3.2 copy-start.14
  73.1 3.4 copy-start.11
  73.1 4.6 copy-start.1
  73.1 236.2 %all-reduce.4.cloned.1.call-start = ((), (), s32[]{:S(2)}) async-start(), calls=%async_computation.3 | async-start | bytes 2359296 | tf_op jit(solution)/shard_map/psum | solution.py:118
  75.8 418.3 %all-gather.8.cloned.1.call-start = ((), (), s32[]{:S(2)}) async-start(), calls=%async_computation.5 | async-start | bytes 38928384 | tf_op jit(solution)/shard_map/all_gather | solution.py:17
  82.7 6.9 copy-start.2
  94.5 6.7 copy-start.18
  362.8 455.3 %all-gather.6.cloned.1.call-start = ((), (), s32[]{:S(2)}) async-start(), calls=%async_computation.4 | async-start | bytes 2433024 | tf_op jit(solution)/shard_map/all_gather | solution.py:254
  526.5 2.6 copy-start.4
  531.9 2.6 copy-start.4
  537.3 2.6 copy-start.4
  542.8 2.6 copy-start.4
  548.2 2.6 copy-start.4
  553.6 2.6 copy-start.4
  559.0 2.6 copy-start.4
  564.5 2.6 copy-start.4
  569.9 2.6 copy-start.4
  575.3 2.6 copy-start.4
  580.7 2.6 copy-start.4
  586.2 2.6 copy-start.4
  591.6 2.6 copy-start.4
  597.0 2.6 copy-start.4
  651.3 2.6 copy-start.4
  691.9 62.9 %copy-start.13 = (f32[72]{0:T(128)S(1)}, f32[72]{0:T(128)}, u32[]{:S(2)}) copy-start(f32[72]{0:T(128)} %param.23) | copy-start | bytes 868
  694.2 123.9 %copy-start.15 = (bf16[1,2304,180]{1,2,0:T(8,128)(2,1)S(1)}, bf16[1,2304,180]{1,2,0:T(8,128)(2,1)}, u32[]{:S(2)}) copy-start(bf16[1,2304,180]{1,2,0:T(8,128)(2,1)} %param.25) | copy-start | bytes 2488324
  773.1 140.5 %reduce-scatter.4.cloned.1.call-start = ((), (), s32[]{:S(2)}) async-start(), calls=%async_computation.6 | async-start | bytes 2433024
  917.8 15.5 %all-to-all-start.1 = ((bf16[8,2,2304]{2,1,0:T(2,128)(2,1)}), bf16[8,2,2304]{2,1,0:T(2,128)(2,1)S(1)}, u32[]{:S(2)}, u32[]{:S(2)}) async-start(bf16[8,2,2304]{2,1,0:T(2,128)(2,1)} %reshape.465), calls=%async_computation.1 | async-start | bytes 147456 | tf_op jit(solution)/shard_map/all_to_all | solution.py:274
  (114 other events, 184.8 us)
Sparse Core Ops, SparseCore 0:
  73.2 117.6 all-reduce.5
  194.2 115.0 all-reduce.3
  362.9 131.1 all-gather.7
  773.3 44.8 all-gather.5
  827.2 86.4 reduce-scatter.3
where the time goes:
time: 946 us; the launch traced here: 942 us
  waiting for transfers between devices  360 us (38%)
  blocking collectives  249 us (26%)
  local copies, waits for them, and re-layouts  164 us (17%)
  other arithmetic  97.8 us (10%)
  matrix products  40.8 us (4%)
  between operations  14.9 us (2%)
    psum x1, waiting for transfers between devices, on_device(): query_sum = lax.psum(query_part, 'col')  117 us
    unnamed x7, waiting for transfers between devices  114 us
    add x31, other arithmetic, combine_parts(): rescale(earlier_part[2], factor_one) + rescale(later_part[2], factor_two)  81.3 us
    all_gather x1, waiting for transfers between devices, merged(): pieces = jax.tree.map(lambda part: lax.all_gather(part, axis), value)  76 us
    psum x1, blocking collectives, on_device(): squares = lax.psum(jnp.sum(residual * residual, axis=1), 'col')  62.3 us
    psum x1, blocking collectives, on_device(): squares_two = lax.psum(jnp.sum(middle_wide * middle_wide, axis=1), 'col')  60.6 us
    psum x1, blocking collectives, on_device(): lax.psum(jnp.dot(moe_normed_f, router_weight, precision=lax.Precision.HIG...  60.4 us
    dynamic_slice x62, local copies, waits for them, and re-layouts, merged(): lax.scan(lambda running, slab: (join(running, slab), None), head, tail)  53.9 us
  transfers between devices with their start and end apart: 6, of which 6 were waited for; matrix products, arithmetic and copies ran while one was open for 4% of the time, Pallas kernels for 0%

commit v1 on v0

--- a/solution.py
+++ b/solution.py
@@ -221,7 +221,8 @@
     attn_out = projected.astype(jnp.bfloat16)
     middle = (residual + residual_scale * attn_out.astype(jnp.float32)).astype(jnp.bfloat16)
     middle_wide = middle.astype(jnp.float32)
-    squares_two = lax.psum(jnp.sum(middle_wide * middle_wide, axis=1), "col")
+    v0 = jnp.sum(middle_wide * middle_wide, axis=1)
+    squares_two = jnp.sum(lax.all_gather(v0, "col"), axis=0)
     scale_two = lax.rsqrt(squares_two / D + norm_epsilon)
     moe_normed_f = middle_wide * scale_two[:, None] * moe_gain[None, :]
     logits = lax.psum(jnp.dot(moe_normed_f, router_weight, precision=lax.Precision.HIGHEST), "col")

time: 946 us -> 905 us (0.957)
  blocking collectives: 249 us -> 210 us
    psum x1 -> x0, blocking collectives: 60.6 us -> none  [on_device(): squares_two = lax.psum(jnp.sum(middle_wide * middle_wide, axis=1), 'col')]
    all_gather x0 -> x1, blocking collectives: none -> 20.6 us  [on_device(): squares_two = jnp.sum(lax.all_gather(v0, 'col'), axis=0)]
where the time goes in v1:
time: 905 us; the launch traced here: 902 us
  waiting for transfers between devices  359 us (40%)
  blocking collectives  210 us (23%)
  local copies, waits for them, and re-layouts  163 us (18%)
  other arithmetic  97.8 us (11%)
  matrix products  40.8 us (5%)
  between operations  14.9 us (2%)
    psum x1, waiting for transfers between devices, on_device(): query_sum = lax.psum(query_part, 'col')  117 us
    unnamed x7, waiting for transfers between devices  114 us
    add x31, other arithmetic, combine_parts(): rescale(earlier_part[2], factor_one) + rescale(later_part[2], factor_two)  81.3 us
    all_gather x1, waiting for transfers between devices, merged(): pieces = jax.tree.map(lambda part: lax.all_gather(part, axis), value)  76 us
    psum x1, blocking collectives, on_device(): squares = lax.psum(jnp.sum(residual * residual, axis=1), 'col')  62.3 us
    psum x1, blocking collectives, on_device(): lax.psum(jnp.dot(moe_normed_f, router_weight, precision=lax.Precision.HIG...  60.5 us
    dynamic_slice x62, local copies, waits for them, and re-layouts, merged(): lax.scan(lambda running, slab: (join(running, slab), None), head, tail)  53.9 us
    all_gather x2, blocking collectives, merged(): pieces = jax.tree.map(lambda part: lax.all_gather(part, axis), value)  50.1 us
  transfers between devices with their start and end apart: 6, of which 6 were waited for; matrix products, arithmetic and copies ran while one was open for 4% of the time, Pallas kernels for 0%

profile of v1, /device:TPU:2, one launch (start us, length us, event | category | flops | bytes accessed | tf_op | source)
XLA Modules:
  0.0 901.8 jit_solution(3761320331663184024)
XLA Ops:
  8.0 62.3 %psum.21 = f32[128]{0:T(128)S(1)} all-reduce(f32[128]{0:T(128)S(1)} %fusion.64), channel_id=1, replica_groups=mesh['row'=8,'col'=32] {'col'}, use_global_device_ids=true, to_apply=%region_1.2 | all-reduce | flops 128 | bytes 1024 | tf_op jit(solution)/shard_map/psum | solution.py:114
  70.3 2.7 convolution_convert_fusion
  77.7 5.0 reshape.462
  82.7 6.9 copy.162
  89.5 5.0 reshape.463
  94.5 6.7 copy.163
  102.5 88.4 %all-reduce.6.cloned.1.call-done = bf16[128,4608]{1,0:T(8,128)(2,1)} async-done(((bf16[128,4608]{1,0:T(8,128)(2,1)}), bf16[128,4608]{1,0:T(8,128)(2,1)}) %all-reduce.6.cloned.1.call-update) | async-done | bytes 1179664
  192.2 117.1 %all-reduce.4.cloned.1.call-done = f32[128,36,64]{0,2,1:T(8,128)} async-done(((f32[128,36,64]{0,2,1:T(8,128)}), f32[128,36,64]{0,2,1:T(8,128)}) %all-reduce.4.cloned.1.call-update) | async-done | bytes 1179664 | tf_op jit(solution)/shard_map/psum | solution.py:118
  310.9 51.9 %while.31 = (s32[]{:T(128)}, f32[9,4,128]{2,1,0:T(4,128)S(1)}, f32[9,4,128]{2,1,0:T(4,128)S(1)}, f32[9,128,256]{2,1,0:T(8,128)}, s32[9]{0:T(128)S(1)}, /*index=5...) while((s32[]{:T(128)}, f32[9,4,128]{2,1,0:T(4,128)S(1)}, ...), condition=%wide.region_16.17_spmd.clone.clone, body=%wide.region_11.16_spmd.clone.clone.sunk | while | flops 69911040 | bytes 5058339 | solution.py:212
  368.0 24.4 %all-gather = f32[288,4,128]{2,1,0:T(4,128)S(1)} all-gather(f32[9,4,128]{2,1,0:T(4,128)S(1)} %get-tuple-element.105), channel_id=2, replica_groups=mesh['row'=8,'col'=32] {'col'}, dimensions={0}, use_global_device_ids=true | all-gather | bytes 608256 | tf_op jit(solution)/shard_map/all_gather | solution.py:17
  392.5 25.6 %all-gather.1 = f32[288,4,128]{2,1,0:T(4,128)S(1)} all-gather(f32[9,4,128]{2,1,0:T(4,128)S(1)} %get-tuple-element.106), channel_id=3, replica_groups=mesh['row'=8,'col'=32] {'col'}, dimensions={0}, use_global_device_ids=true | all-gather | bytes 608256 | tf_op jit(solution)/shard_map/all_gather | solution.py:17
  418.2 76.0 %all-gather.10.cloned.1.call-done = f32[288,128,256]{2,1,0:T(8,128)} async-done(((f32[9,128,256]{2,1,0:T(8,128)}), f32[288,128,256]{2,1,0:T(8,128)}) %all-gather.10.cloned.1.call-update) | async-done | bytes 37748752 | tf_op jit(solution)/shard_map/all_gather | solution.py:17
  496.8 26.9 %slice.93 = f32[279,128,256]{2,1,0:T(8,128)} slice(f32[288,128,256]{2,1,0:T(8,128)} %all-gather.10.cloned.1.call-done), slice={[9:288], [0:128], [0:256]} | slice | bytes 73138176 | tf_op jit(solution)/shard_map/slice | solution.py:19
  523.7 168.2 %while.30 = (s32[]{:T(128)}, f32[9,4,128]{2,1,0:T(4,128)S(1)}, f32[9,4,128]{2,1,0:T(4,128)S(1)}, f32[9,128,256]{1,2,0:T(8,128)}, f32[31,9,4,128]{3,2,1,0:T(4,128...) while((s32[]{:T(128)}, f32[9,4,128]{2,1,0:T(4,128)S(1)}, ...), condition=%wide.region_18.19_spmd, body=%wide.region_17.18_spmd.sunk | while | flops 916994 | bytes 17676496 | solution.py:20
  531.9 2.6 fusion.111
  542.8 2.6 fusion.111
  548.2 2.6 fusion.111
  553.6 2.6 fusion.111
  559.1 2.6 fusion.111
  569.9 2.6 fusion.111
  580.8 2.6 fusion.111
  591.6 2.6 fusion.111
  602.5 2.6 fusion.111
  694.2 20.6 %all-gather.4 = f32[32,1,128]{2,1,0:T(1,128)S(1)} all-gather(f32[1,1,128]{2,1,0:T(1,128)S(1)} %bitcast.165), channel_id=5, replica_groups=mesh['row'=8,'col'=32] {'col'}, dimensions={0}, use_global_device_ids=true | all-gather | bytes 16896 | tf_op jit(solution)/shard_map/all_gather | solution.py:225
  716.6 16.4 %all_to_all.14 = bf16[8,64,72]{2,1,0:T(8,128)(2,1)S(1)} all-to-all(bf16[8,64,72]{2,1,0:T(8,128)(2,1)S(1)} %broadcast_select_fusion), channel_id=1, replica_groups=mesh['row'=8,'col'=32] {'row'}, dimensions={0} | all-to-all | bytes 147456 | tf_op jit(solution)/shard_map/all_to_all | solution.py:249
  733.7 43.9 %all-gather.8.cloned.1.call-done = bf16[1,512,2304]{1,2,0:T(8,128)(2,1)} async-done(((bf16[1,512,72]{1,2,0:T(8,128)(2,1)}), bf16[1,512,2304]{1,2,0:T(8,128)(2,1)}) %all-gather.8.cloned.1.call-update) | async-done | bytes 2359312 | tf_op jit(solution)/shard_map/all_gather | solution.py:255
  777.7 3.0 fusion.36
  780.7 3.4 fusion.33
  787.4 60.5 %psum.23 = f32[128,8]{0,1:T(8,128)S(1)} all-reduce(f32[128,8]{0,1:T(8,128)S(1)} %fusion.70), channel_id=1, replica_groups=mesh['row'=8,'col'=32] {'col'}, use_global_device_ids=true, to_apply=%region_27.28 | all-reduce | flops 1024 | bytes 8192 | tf_op jit(solution)/shard_map/psum | solution.py:228
  847.9 25.3 %reduce-scatter.4.cloned.1.call-done = bf16[72,512]{1,0:T(8,128)(2,1)} async-done(((bf16[2304,512]{1,0:T(8,128)(2,1)}), bf16[72,512]{1,0:T(8,128)(2,1)}) %reduce-scatter.4.cloned.1.call-update) | async-done | bytes 73744
  877.3 7.0 all-to-all-start.1
  884.5 8.3 all-to-all-done.1
  (688 shorter events, 219.2 us)
Async XLA Ops:
  7.2 773.5 %copy-start = (bf16[1,180,2304]{2,1,0:T(8,128)(2,1)S(1)}, bf16[1,180,2304]{2,1,0:T(8,128)(2,1)}, u32[]{:S(2)}) copy-start(bf16[1,180,2304]{2,1,0:T(8,128)(2,1)} %param.27) | copy-start | bytes 2488324
  7.2 183.7 %all-reduce.6.cloned.1.call-start = ((), (), s32[]{:S(2)}) async-start(), calls=%async_computation.7 | async-start | bytes 2359296
  70.3 2.9 copy-start.8
  70.3 2.9 copy-start.12
  73.1 2.9 copy-start.17
  73.1 3.2 copy-start.14
  73.1 3.4 copy-start.11
  73.1 4.6 copy-start.1
  73.1 236.2 %all-reduce.4.cloned.1.call-start = ((), (), s32[]{:S(2)}) async-start(), calls=%async_computation.3 | async-start | bytes 2359296 | tf_op jit(solution)/shard_map/psum | solution.py:118
  75.8 418.3 %all-gather.10.cloned.1.call-start = ((), (), s32[]{:S(2)}) async-start(), calls=%async_computation.5 | async-start | bytes 38928384 | tf_op jit(solution)/shard_map/all_gather | solution.py:17
  82.7 6.9 copy-start.2
  94.5 6.7 copy-start.18
  362.8 414.9 %all-gather.8.cloned.1.call-start = ((), (), s32[]{:S(2)}) async-start(), calls=%async_computation.4 | async-start | bytes 2433024 | tf_op jit(solution)/shard_map/all_gather | solution.py:255
  526.5 2.6 copy-start.4
  531.9 2.6 copy-start.4
  537.3 2.6 copy-start.4
  542.8 2.6 copy-start.4
  548.2 2.6 copy-start.4
  553.6 2.6 copy-start.4
  559.0 2.6 copy-start.4
  564.5 2.6 copy-start.4
  569.9 2.6 copy-start.4
  575.3 2.6 copy-start.4
  580.7 2.6 copy-start.4
  586.2 2.6 copy-start.4
  591.6 2.6 copy-start.4
  597.0 2.6 copy-start.4
  651.3 2.6 copy-start.4
  691.9 22.9 %copy-start.13 = (f32[72]{0:T(128)S(1)}, f32[72]{0:T(128)}, u32[]{:S(2)}) copy-start(f32[72]{0:T(128)} %param.23) | copy-start | bytes 868
  694.2 83.4 %copy-start.15 = (bf16[1,2304,180]{1,2,0:T(8,128)(2,1)S(1)}, bf16[1,2304,180]{1,2,0:T(8,128)(2,1)}, u32[]{:S(2)}) copy-start(bf16[1,2304,180]{1,2,0:T(8,128)(2,1)} %param.25) | copy-start | bytes 2488324
  733.7 139.5 %reduce-scatter.4.cloned.1.call-start = ((), (), s32[]{:S(2)}) async-start(), calls=%async_computation.6 | async-start | bytes 2433024
  877.3 15.5 %all-to-all-start.1 = ((bf16[8,2,2304]{2,1,0:T(2,128)(2,1)}), bf16[8,2,2304]{2,1,0:T(2,128)(2,1)S(1)}, u32[]{:S(2)}, u32[]{:S(2)}) async-start(bf16[8,2,2304]{2,1,0:T(2,128)(2,1)} %reshape.473), calls=%async_computation.1 | async-start | bytes 147456 | tf_op jit(solution)/shard_map/all_to_all | solution.py:275
  (114 other events, 184.8 us)
Sparse Core Ops, SparseCore 0:
  73.2 117.6 all-reduce.5
  194.2 115.0 all-reduce.3
  362.9 131.1 all-gather.9
  733.8 43.8 all-gather.7
  786.7 86.4 reduce-scatter.3
